TPU v7x, 256 devices: a whole 4x4x8 slice. The times are simulated.
256 devices in a mesh: ctx: 32 (over y, x, core), head: 8 (over z).
Axes of the slice: x: 4, y: 4, z: 8, core: 2. Of those that a mesh axis runs over, the one named last changes fastest.
Arguments:
- queries: bfloat16 [8192, 4096], P('ctx', 'head'), may hold values from -6 to 6
- key_rows: bfloat16 [8192, 4096], P('ctx', 'head'), may hold values from -6 to 6
- values: bfloat16 [8192, 4096], P('ctx', 'head'), may hold values from -6 to 6
- log_decay: float32 [8192, 32], P('ctx', 'head'), may hold values from 0 to 1, as said below
- head_gain: bfloat16 [4096], P('head'), may hold values from 0.099609375 to 1.8984375
- out_weight: bfloat16 [3072, 4096], P('ctx', 'head'), may hold values from -0.09375 to 0.09375
- residual: bfloat16 [8192, 3072], P('ctx', 'head'), may hold values from -6 to 6
- norm_gain: bfloat16 [3072], P('head'), may hold values from 0.099609375 to 1.8984375
- router: bfloat16 [3072, 32], replicated, may hold values from -0.21875 to 0.21875
- expert_ids: int32 [8192, 2], P('ctx'), may hold values from 0 to 31, all different within a row; in each aligned block of 256 rows (0 to 255, 256 to 511, ...) at most 24 rows name the same one
- gate_weight: bfloat16 [32, 3072, 5120], P('ctx', None, 'head'), may hold values from -0.109375 to 0.109375
- up_weight: bfloat16 [32, 3072, 5120], P('ctx', None, 'head'), may hold values from -0.109375 to 0.109375
- down_weight: bfloat16 [32, 5120, 3072], P('ctx', 'head'), may hold values from -0.125 to 0.125
Outputs:
- layer_out: float32 [8192, 3072], P('ctx', 'head')
Inputs may be any that keep to these rules, and one draw needn't show every extreme that they name: `log_decay`: amounts by which a head's state decays at a position: the state is multiplied by exp(-value). `expert_ids`: each row names 2 different experts; among the rows of one block of 256 positions no expert is named more than 24 times, a bound that some block reaches.
All inputs are finite; a program needn't handle non-finite values.
Results may differ from a plain program's by a relative error of at most 0.007.
Values may be sent and summed in bfloat16 or wider, within the bound.
No kernel may reach another device: no remote copies, remote signals or barrier semaphores. Data moves between devices by JAX's collectives and lax.ppermute only.
A program may use at most 128 MiB of HBM per device.

v0:
```python
import jax
import jax.numpy as jnp
from jax import lax
from jax.sharding import PartitionSpec as P

HEAD_DIM = 128
TOP = 2
HIGH = lax.Precision.HIGHEST
EPSILON = 1e-05


def combine(earlier, later):
    rows = HEAD_DIM
    decay_late = later[:, rows : rows + 1, 0:1]
    state = decay_late * earlier[:, :rows] + later[:, :rows]
    decay = earlier[:, rows : rows + 1] * later[:, rows : rows + 1]
    pad = jnp.zeros((later.shape[0], later.shape[1] - rows - 1, later.shape[2]), later.dtype)
    return jnp.concatenate([state, decay, pad], axis=1)


def exclusive_scan(packed, axis):
    count, mine = (lax.axis_size(axis), lax.axis_index(axis))
    rows = HEAD_DIM
    identity = jnp.zeros_like(packed).at[:, rows].set(1.0)
    window = packed
    before = identity
    shift = 1
    while shift < count:
        pairs = [(j, j + shift) for j in range(count - shift)]
        got = lax.ppermute(window, axis, pairs)
        got = jnp.where(mine >= shift, got, identity)
        before = combine(got, before)
        if 2 * shift < count:
            window = combine(got, window)
        shift *= 2
    return before[:, :rows]


def on_device(
    queries,
    key_rows,
    values,
    log_decay,
    head_gain,
    out_weight,
    residual,
    norm_gain,
    router,
    expert_ids,
    gate_weight,
    up_weight,
    down_weight,
):
    rows = queries.shape[0]
    heads_here = log_decay.shape[1]
    groups = lax.axis_size("head")
    query_heads = queries.reshape(rows, heads_here, HEAD_DIM)
    key_heads = key_rows.reshape(rows, heads_here, HEAD_DIM)
    value_heads = values.reshape(rows, heads_here, HEAD_DIM)
    cumulative = jnp.cumsum(log_decay, axis=0)
    scores = jnp.einsum("thd,jhd->htj", query_heads, key_heads, preferred_element_type=jnp.float32)
    causal = jnp.arange(rows)[:, None] >= jnp.arange(rows)[None, :]
    gap = cumulative.T[:, :, None] - cumulative.T[:, None, :]
    weight = jnp.where(causal[None], jnp.exp(-jnp.where(causal[None], gap, 0.0)), 0.0)
    weighted = (scores * weight).astype(jnp.bfloat16)
    inner = jnp.einsum("htj,jhd->thd", weighted, value_heads, preferred_element_type=jnp.float32)
    value_wide = value_heads.astype(jnp.float32)
    tail = jnp.exp(cumulative - cumulative[-1:])
    keys_tail = key_heads.astype(jnp.float32) * tail[:, :, None]
    local_state = jnp.einsum("jhd,jhe->hde", keys_tail, value_wide, precision=HIGH)
    shard_decay = jnp.exp(-cumulative[-1])
    decay_rows = jnp.broadcast_to(shard_decay[:, None, None], (heads_here, 1, HEAD_DIM))
    pad = jnp.zeros((heads_here, 7, HEAD_DIM), jnp.float32)
    packed = jnp.concatenate([local_state, decay_rows, pad], axis=1)
    incoming = exclusive_scan(packed, "ctx")
    query_decayed = query_heads.astype(jnp.float32) * jnp.exp(-cumulative)[:, :, None]
    outer = jnp.einsum("thd,hde->the", query_decayed, incoming, precision=HIGH)
    mixed = inner + outer
    mean_sq = jnp.mean(mixed * mixed, axis=-1, keepdims=True)
    gain_heads = head_gain.astype(jnp.float32).reshape(heads_here, HEAD_DIM)
    normed = (
        (mixed * lax.rsqrt(mean_sq + EPSILON) * gain_heads)
        .astype(jnp.bfloat16)
        .reshape(rows, heads_here * HEAD_DIM)
    )
    width = residual.shape[1]
    full = width * groups
    weight_all = lax.all_gather(out_weight, "ctx", axis=0, tiled=True).reshape(
        groups, width, heads_here * HEAD_DIM
    )
    partial_proj = jnp.einsum(
        "tk,gck->gtc", normed, weight_all, preferred_element_type=jnp.float32
    ).astype(jnp.bfloat16)
    total = lax.psum_scatter(partial_proj, "head", scatter_dimension=0, tiled=True)
    stream_mine = residual.astype(jnp.float32) + total[0].astype(jnp.float32)
    sq_part = jnp.sum(stream_mine * stream_mine, axis=1)
    sq_hi = sq_part.astype(jnp.bfloat16)
    sq_lo = (sq_part - sq_hi.astype(jnp.float32)).astype(jnp.bfloat16)
    experts = router.shape[1]
    capacity = 3 * rows * TOP // (2 * experts)
    lane = 128
    wide = width + lane
    other_id = expert_ids[:, ::-1].astype(jnp.bfloat16)
    token_rows = jnp.concatenate(
        [
            stream_mine.astype(jnp.bfloat16),
            sq_hi[:, None],
            sq_lo[:, None],
            jnp.zeros((rows, lane - 2), jnp.bfloat16),
        ],
        axis=1,
    )
    token_rows = jnp.concatenate([token_rows, jnp.zeros((8, wide), jnp.bfloat16)], axis=0)
    flat_ids = expert_ids.reshape(-1)
    onehot = (flat_ids[:, None] == jnp.arange(experts, dtype=jnp.int32)[None, :]).astype(jnp.int32)
    before = jnp.cumsum(onehot, axis=0) - onehot
    position = jnp.sum(before * onehot, axis=1)
    slot = flat_ids * capacity + position
    owner = jnp.arange(rows * TOP, dtype=jnp.int32) // TOP
    slot_token = jnp.full((experts * capacity,), rows, jnp.int32).at[slot].set(owner)
    slot_other = jnp.zeros((experts * capacity,), jnp.bfloat16).at[slot].set(other_id.reshape(-1))
    outgoing = token_rows[slot_token]
    outgoing = outgoing.at[:, width + 2].set(slot_other).reshape(experts, capacity, wide)
    arriving = lax.all_to_all(outgoing, "ctx", split_axis=0, concat_axis=0, tiled=True)
    flat = arriving.reshape(-1, wide)
    slots_here = flat.shape[0]
    sq_rows = jnp.transpose(flat[:, width : width + 2]).reshape(2 * slots_here // width, width)
    spare = 7 - sq_rows.shape[0]
    extra = jnp.concatenate(
        [norm_gain[None, :], sq_rows, jnp.zeros((spare, width), jnp.bfloat16)], axis=0
    )
    gathered = lax.all_gather(jnp.concatenate([flat[:, :width], extra], axis=0), "head", axis=0)
    stream_blocks = gathered[:, :slots_here].astype(jnp.float32)
    gain_blocks = gathered[:, slots_here].astype(jnp.float32)
    sq_parts = gathered[:, slots_here + 1 : slots_here + 1 + sq_rows.shape[0]].astype(jnp.float32)
    sq_parts = sq_parts.reshape(groups, 2, slots_here)
    stream_sq = jnp.sum(sq_parts, axis=(0, 1))[None, :, None] / full
    other_here = flat[:, width + 2].astype(jnp.int32)
    moe_in = (stream_blocks * lax.rsqrt(stream_sq + EPSILON) * gain_blocks[:, None, :]).astype(
        jnp.bfloat16
    )
    router_blocks = router.reshape(groups, width, router.shape[1])
    logits = jnp.einsum("grc,gce->re", moe_in, router_blocks, preferred_element_type=jnp.float32)
    expert_here = lax.axis_index("ctx")
    names = jnp.arange(experts, dtype=jnp.int32)[None, :]
    own_logit = jnp.sum(jnp.where(names == expert_here, logits, 0.0), axis=1)
    other_logit = jnp.sum(jnp.where(names == other_here[:, None], logits, 0.0), axis=1)
    mix_here = jax.nn.sigmoid(own_logit - other_logit)
    mix_hi = mix_here.astype(jnp.bfloat16)
    mix_lo = (mix_here - mix_hi.astype(jnp.float32)).astype(jnp.bfloat16)
    hidden = gate_weight.shape[2]
    gate = jnp.einsum(
        "grc,gcf->rf",
        moe_in,
        gate_weight[0].reshape(groups, width, hidden),
        preferred_element_type=jnp.float32,
    )
    up = jnp.einsum(
        "grc,gcf->rf",
        moe_in,
        up_weight[0].reshape(groups, width, hidden),
        preferred_element_type=jnp.float32,
    )
    activated = (jax.nn.silu(gate) * up).astype(jnp.bfloat16)
    down = down_weight[0].reshape(down_weight.shape[1], groups, width)
    partial_value = jnp.einsum(
        "rf,fgc->grc", activated, down, preferred_element_type=jnp.float32
    ).astype(jnp.bfloat16)
    summed = lax.psum_scatter(partial_value, "head", scatter_dimension=0, tiled=True)[0]
    back = jnp.concatenate(
        [summed, mix_hi[:, None], mix_lo[:, None], jnp.zeros((slots_here, lane - 2), jnp.bfloat16)],
        axis=1,
    ).reshape(arriving.shape[0], arriving.shape[1], wide)
    returned = lax.all_to_all(back, "ctx", split_axis=0, concat_axis=0, tiled=True)
    picked_rows = returned.reshape(experts * capacity, wide)[slot].astype(jnp.float32)
    picked_rows = picked_rows.reshape(rows, TOP, wide)
    mix_weights = picked_rows[:, :, width] + picked_rows[:, :, width + 1]
    moe_out = jnp.sum(picked_rows[:, :, :width] * mix_weights[:, :, None], axis=1)
    return stream_mine + moe_out


def solution(mesh):
    placed = (
        P("ctx", "head"),
        P("ctx", "head"),
        P("ctx", "head"),
        P("ctx", "head"),
        P("head"),
        P("ctx", "head"),
        P("ctx", "head"),
        P("head"),
        P(),
        P("ctx", None),
        P("ctx", None, "head"),
        P("ctx", None, "head"),
        P("ctx", "head", None),
    )
    return jax.shard_map(
        on_device, mesh=mesh, in_specs=placed, out_specs=P("ctx", "head"), check_vma=False
    )
```

profile of v0, /device:TPU:1, one launch (start us, length us, event | category | flops | bytes accessed | tf_op | source)
XLA Modules:
  0.0 318.7 jit_solution(5503128526121776230)
XLA Ops:
  10.4 1.3 fusion.20
  11.9 4.5 %collective-permute-start = (f32[4,136,128]{2,1,0:T(8,128)S(1)}, f32[4,136,128]{2,1,0:T(8,128)S(1)}, u32[]{:S(2)}, u32[]{:S(2)}) collective-permute-start(f32[4,136,128]{2,1,0:T(8,128)S(1)} %maximum_maximum_fusion.2), channel_id=1, source_target_pairs={{0,8},{8,16},{16,24},{24,32},{32,40},{40,48},{48,56},{56,64},{64,7... | collective-permute-start | bytes 835592 | tf_op jit(solution)/shard_map/ppermute | solution.py:30
  16.5 3.4 %collective-permute-done = f32[4,136,128]{2,1,0:T(8,128)S(1)} collective-permute-done((f32[4,136,128]{2,1,0:T(8,128)S(1)}, f32[4,136,128]{2,1,0:T(8,128)S(1)}, u32[]{:S(2)}, u32[]{:S(2)}) %collective-permute-start) | collective-permute-done | bytes 278560 | tf_op jit(solution)/shard_map/ppermute | solution.py:30
  20.2 3.1 collective-permute-start.1
  23.5 4.4 %collective-permute-done.1 = f32[4,136,128]{2,1,0:T(8,128)S(1)} collective-permute-done((f32[4,136,128]{2,1,0:T(8,128)S(1)}, f32[4,136,128]{2,1,0:T(8,128)S(1)}, u32[]{:S(2)}, u32[]{:S(2)}) %collective-permute-start.1) | collective-permute-done | bytes 278560 | tf_op jit(solution)/shard_map/ppermute | solution.py:30
  28.2 5.1 %collective-permute-start.2 = (f32[4,136,128]{2,1,0:T(8,128)S(1)}, f32[4,136,128]{2,1,0:T(8,128)S(1)}, u32[]{:S(2)}, u32[]{:S(2)}) collective-permute-start(f32[4,136,128]{2,1,0:T(8,128)S(1)} %maximum_maximum_fusion.4), channel_id=1, source_target_pairs={{0,32},{8,40},{16,48},{24,56},{32,64},{40,72},{48,80},{56,88},{64,... | collective-permute-start | bytes 835592 | tf_op jit(solution)/shard_map/ppermute | solution.py:30
  34.0 3.2 %collective-permute-done.2 = f32[4,136,128]{2,1,0:T(8,128)S(1)} collective-permute-done((f32[4,136,128]{2,1,0:T(8,128)S(1)}, f32[4,136,128]{2,1,0:T(8,128)S(1)}, u32[]{:S(2)}, u32[]{:S(2)}) %collective-permute-start.2) | collective-permute-done | bytes 278560 | tf_op jit(solution)/shard_map/ppermute | solution.py:30
  37.5 5.9 %collective-permute-start.3 = (f32[4,136,128]{2,1,0:T(8,128)S(1)}, f32[4,136,128]{2,1,0:T(8,128)S(1)}, u32[]{:S(2)}, u32[]{:S(2)}) collective-permute-start(f32[4,136,128]{2,1,0:T(8,128)S(1)} %maximum_maximum_fusion.5), channel_id=1, source_target_pairs={{0,64},{8,72},{16,80},{24,88},{32,96},{40,104},{48,112},{56,120},{... | collective-permute-start | bytes 835592 | tf_op jit(solution)/shard_map/ppermute | solution.py:30
  43.6 3.9 %collective-permute-done.3 = f32[4,136,128]{2,1,0:T(8,128)S(1)} collective-permute-done((f32[4,136,128]{2,1,0:T(8,128)S(1)}, f32[4,136,128]{2,1,0:T(8,128)S(1)}, u32[]{:S(2)}, u32[]{:S(2)}) %collective-permute-start.3) | collective-permute-done | bytes 278560 | tf_op jit(solution)/shard_map/ppermute | solution.py:30
  47.7 5.4 %collective-permute-start.4 = (f32[4,136,128]{2,1,0:T(8,128)S(1)}, f32[4,136,128]{2,1,0:T(8,128)S(1)}, u32[]{:S(2)}, u32[]{:S(2)}) collective-permute-start(f32[4,136,128]{2,1,0:T(8,128)S(1)} %maximum_maximum_fusion.6), channel_id=1, source_target_pairs={{0,128},{8,136},{16,144},{24,152},{32,160},{40,168},{48,176},{56,1... | collective-permute-start | bytes 835592 | tf_op jit(solution)/shard_map/ppermute | solution.py:30
  53.5 3.1 collective-permute-done.4
  57.6 15.2 %all-gather.4.cloned.1.call-done = bf16[3072,512]{1,0:T(8,128)(2,1)} async-done(((bf16[96,512]{1,0:T(8,128)(2,1)}), bf16[3072,512]{1,0:T(8,128)(2,1)}) %all-gather.4.cloned.1.call-update) | async-done | bytes 3145744 | tf_op jit(solution)/shard_map/all_gather | solution.py:88
  72.8 4.1 %fusion.8 = bf16[8,256,384]{2,1,0:T(8,128)(2,1)} fusion(bf16[256,512,1]{0,1,2:T(8,128)(2,1)S(1)} %bitcast.154, bf16[8,384,512]{2,1,0:T(8,128)(2,1)} %bitcast.153), kind=kOutput, calls=%fused_computation.16 | convolution fusion | flops 806092800 | bytes 4980736 | tf_op jit(solution)/shard_map/tk,gck->gtc/dot_general | solution.py:91
  79.7 3.8 %scatter_custom_fusion.1 = bf16[768]{0:T(1024)(128)(2,1)S(1)} fusion(s32[512]{0:T(512)S(1)} %bitcast.165, bf16[512]{0:T(512)(128)(2,1)S(1)} %reshape.350, bf16[]{:T(256)} %constant.126.clone.1), kind=kCustom, calls=%fused_computation.150 | custom fusion | bytes 1538 | tf_op jit(solution)/shard_map/scatter | solution.py:121
  83.4 2.4 scatter_custom_fusion
  86.5 27.3 %reduce-scatter.3.cloned.1.call-done = bf16[1,256,384]{2,1,0:T(8,128)(2,1)} async-done(((bf16[8,256,384]{2,1,0:T(8,128)(2,1)}), bf16[1,256,384]{2,1,0:T(8,128)(2,1)}) %reduce-scatter.3.cloned.1.call-update) | async-done | bytes 196624 | tf_op jit(solution)/shard_map/reduce_scatter | solution.py:94
  115.4 3.3 %gather_fusion = bf16[768,512]{1,0:T(8,128)(2,1)} fusion(bf16[264,512]{1,0:T(8,128)(2,1)S(1)} %concatenate.40, s32[1024]{0:T(1024)S(1)} %pad_clamp_fusion.1), kind=kCustom, calls=%fused_computation | custom fusion | bytes 1575936 | tf_op jit(solution)/shard_map/gather | solution.py:122
  118.7 1.8 slice_select_fusion.1
  120.5 2.2 scatter.24
  122.8 11.6 %all-to-all-start = ((bf16[32,24,512]{2,1,0:T(8,128)(2,1)}), bf16[32,24,512]{2,1,0:T(8,128)(2,1)S(1)}, u32[]{:S(2)}, u32[]{:S(2)}) async-start(bf16[32,24,512]{2,1,0:T(8,128)(2,1)} %bitcast.15), calls=%async_computation.1 | async-start | bytes 1572864 | tf_op jit(solution)/shard_map/all_to_all | solution.py:124
  134.6 14.1 %all-to-all-done = bf16[32,24,512]{2,1,0:T(8,128)(2,1)S(1)} async-done(((bf16[32,24,512]{2,1,0:T(8,128)(2,1)}), bf16[32,24,512]{2,1,0:T(8,128)(2,1)S(1)}, u32[]{:S(2)}, u32[]{:S(2)}) %all-to-all-start) | async-done | bytes 786464 | tf_op jit(solution)/shard_map/all_to_all | solution.py:124
  150.0 5.0 %copy.212 = bf16[80,8,8,384]{3,2,1,0:T(8,128)(2,1)} copy(bf16[80,8,8,384]{3,1,2,0:T(8,128)(2,1)} %bitcast.151) | data formatting | bytes 7864320
  155.0 50.2 %all-gather.6.cloned.1.call-done = bf16[6208,384]{1,0:T(8,128)(2,1)} async-done(((bf16[776,384]{1,0:T(8,128)(2,1)}), bf16[6208,384]{1,0:T(8,128)(2,1)}) %all-gather.6.cloned.1.call-update) | async-done | bytes 4767760 | tf_op jit(solution)/shard_map/all_gather | solution.py:132
  206.9 7.2 %fusion.76 = f32[768,640,1]{1,0,2:T(8,128)S(1)} fusion(bf16[8,384,640]{2,1,0:T(8,128)(2,1)} %bitcast.176, bf16[8,776,384]{2,1,0:T(8,128)(2,1)} %bitcast.173, f32[8,384]{1,0:T(8,128)S(1)} %bitcast.158, f32[768]{0:T(1024)S(1)} %add_rsqrt_fusion), kind=kOutput, calls=%fused_computation.159 | convolution fusion | flops 3029336064 | bytes 10632192 | tf_op jit(solution)/shard_map/grc,gcf->rf/dot_general | solution.py:152
  214.2 4.0 %fusion.9 = bf16[768,640,1]{1,0,2:T(8,128)(2,1)S(1)} fusion(bf16[8,384,640]{2,1,0:T(8,128)(2,1)S(1)} %bitcast.177, f32[768,640,1]{1,0,2:T(8,128)S(1)} %fusion.76, bf16[8,776,384]{2,1,0:T(8,128)(2,1)S(1)} %bitcast.175, f32[8,384]{1,0:T(8,128)S(1)} %bitcast.159, f32[768]{0:T(1024)S(1)} %add_rsqrt_fusion), kind=kOutput, calls=%fused_computation.18 | convolution fusion | flops 3032285184 | bytes 11616256 | tf_op jit(solution)/shard_map/grc,gcf->rf/dot_general | solution.py:158
  218.2 5.6 %convert_bitcast_fusion = bf16[8,768,384]{2,1,0:T(8,128)(2,1)} fusion(bf16[768,640,1]{1,0,2:T(8,128)(2,1)S(1)} %fusion.9, bf16[640,8,384]{2,1,0:T(8,128)(2,1)S(1)} %bitcast.152), kind=kOutput, calls=%fused_computation.5 | convolution fusion | flops 3022258176 | bytes 9633792 | tf_op jit(solution)/shard_map/rf,fgc->grc/dot_general | solution.py:166
  224.7 4.0 %select_reduce_fusion = (f32[768]{0:T(1024)S(1)}, f32[768]{0:T(1024)S(1)}) fusion(s32[768]{0:T(1024)S(1)} %convert_reduce_fusion, pred[32]{0:T(512)(128)(4,1)S(1)} %iota_compare_fusion.4, bf16[4,8,8,384]{3,2,1,0:T(8,128)(2,1)S(1)} %bitcast.178, bf16[8,776,384]{2,1,0:T(8,128)(2,1)} %bitcast.174, f32[8,384]{1,0:T(8,128)S(1)} %bitcast.160, ...), kind=kOutput, calls=%fused_computation.97 | convolution fusion | flops 160553472 | bytes 4939808 | tf_op jit(solution)/shard_map/grc,gce->re/dot_general | solution.py:143
  229.4 53.5 %reduce-scatter.5.cloned.1.call-done = bf16[1,768,384]{2,1,0:T(8,128)(2,1)} async-done(((bf16[8,768,384]{2,1,0:T(8,128)(2,1)}), bf16[1,768,384]{2,1,0:T(8,128)(2,1)}) %reduce-scatter.5.cloned.1.call-update) | async-done | bytes 589840 | tf_op jit(solution)/shard_map/reduce_scatter | solution.py:169
  283.0 2.2 maximum_maximum_fusion
  285.1 7.6 %all-to-all-start.1 = ((bf16[32,24,512]{2,1,0:T(8,128)(2,1)}), bf16[32,24,512]{2,1,0:T(8,128)(2,1)S(1)}, u32[]{:S(2)}, u32[]{:S(2)}) async-start(bf16[32,24,512]{2,1,0:T(8,128)(2,1)} %maximum_maximum_fusion), calls=%async_computation.3 | async-start | bytes 1572864 | tf_op jit(solution)/shard_map/all_to_all | solution.py:174
  292.8 14.2 %all-to-all-done.1 = bf16[32,24,512]{2,1,0:T(8,128)(2,1)S(1)} async-done(((bf16[32,24,512]{2,1,0:T(8,128)(2,1)}), bf16[32,24,512]{2,1,0:T(8,128)(2,1)S(1)}, u32[]{:S(2)}, u32[]{:S(2)}) %all-to-all-start.1) | async-done | bytes 786464 | tf_op jit(solution)/shard_map/all_to_all | solution.py:174
  307.0 2.0 gather_fusion.1
  (138 shorter events, 20.2 us)
Async XLA Ops:
  6.5 26.8 %copy-start = (bf16[256,512]{1,0:T(8,128)(2,1)S(1)}, bf16[256,512]{1,0:T(8,128)(2,1)}, u32[]{:S(2)}) copy-start(bf16[256,512]{1,0:T(8,128)(2,1)} %param.17) | copy-start | bytes 786436
  6.5 21.4 %copy-start.1 = (f32[4,136,128]{2,1,0:T(8,128)S(1)}, f32[4,136,128]{2,1,0:T(8,128)}, u32[]{:S(2)}) copy-start(f32[4,136,128]{2,1,0:T(8,128)} %constant.121.clone.1) | copy-start | bytes 835588
  6.5 26.8 %copy-start.5 = (bf16[256,512]{1,0:T(8,128)(2,1)S(1)}, bf16[256,512]{1,0:T(8,128)(2,1)}, u32[]{:S(2)}) copy-start(bf16[256,512]{1,0:T(8,128)(2,1)} %param.19) | copy-start | bytes 786436
  6.5 66.2 %all-gather.4.cloned.1.call-start = ((), (), s32[]{:S(2)}) async-start(), calls=%async_computation.4 | async-start | bytes 3244032 | tf_op jit(solution)/shard_map/all_gather | solution.py:88
  11.9 8.0 %collective-permute-start = (f32[4,136,128]{2,1,0:T(8,128)S(1)}, f32[4,136,128]{2,1,0:T(8,128)S(1)}, u32[]{:S(2)}, u32[]{:S(2)}) collective-permute-start(f32[4,136,128]{2,1,0:T(8,128)S(1)} %maximum_maximum_fusion.2), channel_id=1, source_target_pairs={{0,8},{8,16},{16,24},{24,32},{32,40},{40,48},{48,56},{56,64},{64,7... | collective-permute-start | bytes 835592 | tf_op jit(solution)/shard_map/ppermute | solution.py:30
  16.4 97.5 %reduce-scatter.3.cloned.1.call-start = ((), (), s32[]{:S(2)}) async-start(), calls=%async_computation.5 | async-start | bytes 1769472 | tf_op jit(solution)/shard_map/reduce_scatter | solution.py:94
  20.2 23.3 %copy-start.7 = (bf16[512]{0:T(512)(128)(2,1)S(1)}, bf16[512]{0:T(512)(128)(2,1)}, u32[]{:S(2)}) copy-start(bf16[512]{0:T(512)(128)(2,1)} %param.21) | copy-start | bytes 3076
  20.2 7.7 %collective-permute-start.1 = (f32[4,136,128]{2,1,0:T(8,128)S(1)}, f32[4,136,128]{2,1,0:T(8,128)S(1)}, u32[]{:S(2)}, u32[]{:S(2)}) collective-permute-start(f32[4,136,128]{2,1,0:T(8,128)S(1)} %maximum_maximum_fusion.3), channel_id=1, source_target_pairs={{0,16},{8,24},{16,32},{24,40},{32,48},{40,56},{48,64},{56,72},{64,... | collective-permute-start | bytes 835592 | tf_op jit(solution)/shard_map/ppermute | solution.py:30
  28.2 9.1 %collective-permute-start.2 = (f32[4,136,128]{2,1,0:T(8,128)S(1)}, f32[4,136,128]{2,1,0:T(8,128)S(1)}, u32[]{:S(2)}, u32[]{:S(2)}) collective-permute-start(f32[4,136,128]{2,1,0:T(8,128)S(1)} %maximum_maximum_fusion.4), channel_id=1, source_target_pairs={{0,32},{8,40},{16,48},{24,56},{32,64},{40,72},{48,80},{56,88},{64,... | collective-permute-start | bytes 835592 | tf_op jit(solution)/shard_map/ppermute | solution.py:30
  37.5 9.9 %collective-permute-start.3 = (f32[4,136,128]{2,1,0:T(8,128)S(1)}, f32[4,136,128]{2,1,0:T(8,128)S(1)}, u32[]{:S(2)}, u32[]{:S(2)}) collective-permute-start(f32[4,136,128]{2,1,0:T(8,128)S(1)} %maximum_maximum_fusion.5), channel_id=1, source_target_pairs={{0,64},{8,72},{16,80},{24,88},{32,96},{40,104},{48,112},{56,120},{... | collective-permute-start | bytes 835592 | tf_op jit(solution)/shard_map/ppermute | solution.py:30
  47.7 8.9 %collective-permute-start.4 = (f32[4,136,128]{2,1,0:T(8,128)S(1)}, f32[4,136,128]{2,1,0:T(8,128)S(1)}, u32[]{:S(2)}, u32[]{:S(2)}) collective-permute-start(f32[4,136,128]{2,1,0:T(8,128)S(1)} %maximum_maximum_fusion.6), channel_id=1, source_target_pairs={{0,128},{8,136},{16,144},{24,152},{32,160},{40,168},{48,176},{56,1... | collective-permute-start | bytes 835592 | tf_op jit(solution)/shard_map/ppermute | solution.py:30
  57.4 19.4 %copy-start.6 = (s32[256,2]{0,1:T(2,128)S(1)}, s32[256,2]{0,1:T(2,128)}, u32[]{:S(2)}) copy-start(s32[256,2]{0,1:T(2,128)} %param.26) | copy-start | bytes 6148
  57.6 56.3 %copy-start.3 = (bf16[256,384]{1,0:T(8,128)(2,1)S(1)}, bf16[256,384]{1,0:T(8,128)(2,1)}, u32[]{:S(2)}) copy-start(bf16[256,384]{1,0:T(8,128)(2,1)} %param.23) | copy-start | bytes 589828
  115.4 19.0 %copy-start.8 = (bf16[384]{0:T(512)(128)(2,1)S(1)}, bf16[384]{0:T(512)(128)(2,1)}, u32[]{:S(2)}) copy-start(bf16[384]{0:T(512)(128)(2,1)} %param.24) | copy-start | bytes 2308
  122.8 25.9 %all-to-all-start = ((bf16[32,24,512]{2,1,0:T(8,128)(2,1)}), bf16[32,24,512]{2,1,0:T(8,128)(2,1)S(1)}, u32[]{:S(2)}, u32[]{:S(2)}) async-start(bf16[32,24,512]{2,1,0:T(8,128)(2,1)} %bitcast.15), calls=%async_computation.1 | async-start | bytes 1572864 | tf_op jit(solution)/shard_map/all_to_all | solution.py:124
  134.4 70.8 %all-gather.6.cloned.1.call-start = ((), (), s32[]{:S(2)}) async-start(), calls=%async_computation.7 | async-start | bytes 5363712 | tf_op jit(solution)/shard_map/all_gather | solution.py:132
  150.0 133.0 %reduce-scatter.5.cloned.1.call-start = ((), (), s32[]{:S(2)}) async-start(), calls=%async_computation.6 | async-start | bytes 5308416 | tf_op jit(solution)/shard_map/reduce_scatter | solution.py:169
  206.9 7.3 %copy-start.9 = (bf16[6208,384]{1,0:T(8,128)(2,1)S(1)}, bf16[6208,384]{1,0:T(8,128)(2,1)}, u32[]{:S(2)}) copy-start(bf16[6208,384]{1,0:T(8,128)(2,1)} %all-gather.6.cloned.1.call-done) | copy-start | bytes 14303236
  206.9 7.3 %copy-start.10 = (bf16[1,3072,640]{2,1,0:T(8,128)(2,1)S(1)}, bf16[1,3072,640]{2,1,0:T(8,128)(2,1)}, u32[]{:S(2)}) copy-start(bf16[1,3072,640]{2,1,0:T(8,128)(2,1)} %param.28) | copy-start | bytes 11796484
  214.1 4.0 %copy-start.2 = (bf16[80,8,8,384]{3,2,1,0:T(8,128)(2,1)S(1)}, bf16[80,8,8,384]{3,2,1,0:T(8,128)(2,1)}, u32[]{:S(2)}) copy-start(bf16[80,8,8,384]{3,2,1,0:T(8,128)(2,1)} %copy.212) | copy-start | bytes 11796484
  223.8 0.9 copy-start.11
  285.1 21.8 %all-to-all-start.1 = ((bf16[32,24,512]{2,1,0:T(8,128)(2,1)}), bf16[32,24,512]{2,1,0:T(8,128)(2,1)S(1)}, u32[]{:S(2)}, u32[]{:S(2)}) async-start(bf16[32,24,512]{2,1,0:T(8,128)(2,1)} %maximum_maximum_fusion), calls=%async_computation.3 | async-start | bytes 1572864 | tf_op jit(solution)/shard_map/all_to_all | solution.py:174
  307.0 4.4 %copy-start.4 = (bf16[1,256,384]{2,1,0:T(8,128)(2,1)S(1)}, bf16[1,256,384]{2,1,0:T(8,128)(2,1)}, u32[]{:S(2)}) copy-start(bf16[1,256,384]{2,1,0:T(8,128)(2,1)} %reduce-scatter.3.cloned.1.call-done) | copy-start | bytes 589828
Sparse Core Ops, SparseCore 0:
  16.5 56.1 all-gather.3
  77.0 36.8 reduce-scatter.2
  150.1 55.0 all-gather.5
  224.0 58.9 reduce-scatter.4
where the time goes:
time: 320 us; the launch traced here: 319 us
  waiting for transfers between devices  193 us (60%)
  starting transfers between devices  43.4 us (14%)
  matrix products  27.7 us (9%)
  local copies, waits for them, and re-layouts  26.6 us (8%)
  other arithmetic  14.7 us (5%)
  between operations  13.8 us (4%)
    reduce_scatter x1, waiting for transfers between devices, on_device(): lax.psum_scatter(partial_value, 'head', scatter_dimension=0, tiled=True)[0]  53.5 us
    all_gather x1, waiting for transfers between devices, on_device(): lax.all_gather(jnp.concatenate([flat[:, :width], extra], axis=0), 'head',...  50.2 us
    reduce_scatter x1, waiting for transfers between devices, on_device(): lax.psum_scatter(partial_proj, 'head', scatter_dimension=0, tiled=True)  27.3 us
    ppermute x5, starting transfers between devices, exclusive_scan(): got = lax.ppermute(window, axis, pairs)  24.1 us
    ppermute x5, waiting for transfers between devices, exclusive_scan(): got = lax.ppermute(window, axis, pairs)  18 us
    all_gather x1, waiting for transfers between devices, on_device(): lax.all_gather(out_weight, 'ctx', axis=0, tiled=True)  15.2 us
    all_to_all x1, waiting for transfers between devices, on_device(): lax.all_to_all(back, 'ctx', split_axis=0, concat_axis=0, tiled=True)  14.2 us
    all_to_all x1, waiting for transfers between devices, on_device(): lax.all_to_all(outgoing, 'ctx', split_axis=0, concat_axis=0, tiled=True)  14.1 us
  transfers between devices with their start and end apart: 11, of which 11 were waited for; matrix products, arithmetic and copies ran while one was open for 7% of the time, Pallas kernels for 0%

commit v1 on v0

--- a/solution.py
+++ b/solution.py
@@ -7,6 +7,12 @@
 TOP = 2
 HIGH = lax.Precision.HIGHEST
 EPSILON = 1e-05
+
+
+def pass_map_over_axis(local_x, dim_at):
+    return jnp.concatenate(
+        lax.all_to_all(jnp.stack([local_x] * lax.axis_size("ctx"), 0), "ctx", 0, 0), dim_at
+    )
 
 
 def combine(earlier, later):
@@ -85,9 +91,7 @@
     )
     width = residual.shape[1]
     full = width * groups
-    weight_all = lax.all_gather(out_weight, "ctx", axis=0, tiled=True).reshape(
-        groups, width, heads_here * HEAD_DIM
-    )
+    weight_all = pass_map_over_axis(out_weight, 0).reshape(groups, width, heads_here * HEAD_DIM)
     partial_proj = jnp.einsum(
         "tk,gck->gtc", normed, weight_all, preferred_element_type=jnp.float32
     ).astype(jnp.bfloat16)

time: 320 us -> 356 us (1.11)
  starting transfers between devices: 43.4 us -> 55.4 us
  waiting for transfers between devices: 193 us -> 203 us
  other arithmetic: 14.7 us -> 23.2 us
  local copies, waits for them, and re-layouts: 26.6 us -> 30.8 us
    ppermute x5, waiting for transfers between devices: 18 us -> 40.3 us  [exclusive_scan(): got = lax.ppermute(window, axis, pairs)]
    all_gather x1 -> x0, waiting for transfers between devices: 15.2 us -> none  [on_device(): lax.all_gather(out_weight, 'ctx', axis=0, tiled=True)]
    all_to_all x0 -> x1, starting transfers between devices: none -> 9.59 us  [pass_map_over_axis(): lax.all_to_all(jnp.stack([local_x] * lax.axis_size('ctx'), 0), 'ctx', 0, 0)]
    unnamed x30 -> x46, local copies, waits for them, and re-layouts: 6.05 us -> 8.05 us
  transfers between devices with their start and end apart: 11 -> 11, of which waited for: 11 -> 9; matrix products, arithmetic and copies ran while one was open for 7% -> 10% of each run, Pallas kernels for 0% -> 0%
where the time goes in v1:
time: 356 us; the launch traced here: 354 us
  waiting for transfers between devices  203 us (57%)
  starting transfers between devices  55.4 us (16%)
  local copies, waits for them, and re-layouts  30.8 us (9%)
  matrix products  28.6 us (8%)
  other arithmetic  23.2 us (7%)
  between operations  13.8 us (4%)
    reduce_scatter x1, waiting for transfers between devices, on_device(): lax.psum_scatter(partial_value, 'head', scatter_dimension=0, tiled=True)[0]  53.6 us
    all_gather x1, waiting for transfers between devices, on_device(): lax.all_gather(jnp.concatenate([flat[:, :width], extra], axis=0), 'head',...  50 us
    ppermute x5, waiting for transfers between devices, exclusive_scan(): got = lax.ppermute(window, axis, pairs)  40.3 us
    reduce_scatter x1, waiting for transfers between devices, on_device(): lax.psum_scatter(partial_proj, 'head', scatter_dimension=0, tiled=True)  30.4 us
    ppermute x5, starting transfers between devices, exclusive_scan(): got = lax.ppermute(window, axis, pairs)  26.7 us
    all_to_all x1, waiting for transfers between devices, on_device(): lax.all_to_all(back, 'ctx', split_axis=0, concat_axis=0, tiled=True)  14.2 us
    all_to_all x1, waiting for transfers between devices, on_device(): lax.all_to_all(outgoing, 'ctx', split_axis=0, concat_axis=0, tiled=True)  14.1 us
    all_to_all x1, starting transfers between devices, on_device(): lax.all_to_all(outgoing, 'ctx', split_axis=0, concat_axis=0, tiled=True)  11.4 us
  transfers between devices with their start and end apart: 11, of which 9 were waited for; matrix products, arithmetic and copies ran while one was open for 10% of the time, Pallas kernels for 0%

profile of v1, /device:TPU:1, one launch (start us, length us, event | category | flops | bytes accessed | tf_op | source)
XLA Modules:
  0.0 354.3 jit_solution(10889802590736705923)
XLA Ops:
  11.9 4.5 %collective-permute-start = (f32[4,136,128]{2,1,0:T(8,128)S(1)}, f32[4,136,128]{2,1,0:T(8,128)S(1)}, u32[]{:S(2)}, u32[]{:S(2)}) collective-permute-start(f32[4,136,128]{2,1,0:T(8,128)S(1)} %maximum_maximum_fusion.2), channel_id=1, source_target_pairs={{0,8},{8,16},{16,24},{24,32},{32,40},{40,48},{48,56},{56,64},{64,7... | collective-permute-start | bytes 835592 | tf_op jit(solution)/shard_map/ppermute | solution.py:36
  16.4 3.5 collective-permute-done
  22.2 3.8 %collective-permute-start.1 = (f32[4,136,128]{2,1,0:T(8,128)}, f32[4,136,128]{2,1,0:T(8,128)}, u32[]{:S(2)}, u32[]{:S(2)}) collective-permute-start(f32[4,136,128]{2,1,0:T(8,128)} %maximum_maximum_fusion.3), channel_id=1, source_target_pairs={{0,16},{8,24},{16,32},{24,40},{32,48},{40,56},{48,64},{56,72},{64,... | collective-permute-start | bytes 835592 | tf_op jit(solution)/shard_map/ppermute | solution.py:36
  26.0 2.0 stack.2
  28.0 9.6 %all-to-all-start = ((bf16[32,96,512]{2,1,0:T(8,128)(2,1)}), bf16[32,96,512]{2,1,0:T(8,128)(2,1)S(1)}, u32[]{:S(2)}, u32[]{:S(2)}) async-start(bf16[32,96,512]{2,1,0:T(8,128)(2,1)} %stack.2), calls=%async_computation | async-start | bytes 6291456 | tf_op jit(solution)/shard_map/all_to_all | solution.py:14
  42.2 5.5 %collective-permute-start.2 = (f32[4,136,128]{2,1,0:T(8,128)}, f32[4,136,128]{2,1,0:T(8,128)}, u32[]{:S(2)}, u32[]{:S(2)}) collective-permute-start(f32[4,136,128]{2,1,0:T(8,128)} %maximum_maximum_fusion.4), channel_id=1, source_target_pairs={{0,32},{8,40},{16,48},{24,56},{32,64},{40,72},{48,80},{56,88},{64,... | collective-permute-start | bytes 835592 | tf_op jit(solution)/shard_map/ppermute | solution.py:36
  47.7 2.4 convolution_bitcast_fusion.1
  50.3 28.2 %collective-permute-done.2 = f32[4,136,128]{2,1,0:T(8,128)} collective-permute-done((f32[4,136,128]{2,1,0:T(8,128)}, f32[4,136,128]{2,1,0:T(8,128)}, u32[]{:S(2)}, u32[]{:S(2)}) %collective-permute-start.2) | collective-permute-done | bytes 278560 | tf_op jit(solution)/shard_map/ppermute | solution.py:36
  81.3 7.7 %collective-permute-start.3 = (f32[4,136,128]{2,1,0:T(8,128)S(1)}, f32[4,136,128]{2,1,0:T(8,128)S(1)}, u32[]{:S(2)}, u32[]{:S(2)}) collective-permute-start(f32[4,136,128]{2,1,0:T(8,128)S(1)} %maximum_maximum_fusion.5), channel_id=1, source_target_pairs={{0,64},{8,72},{16,80},{24,88},{32,96},{40,104},{48,112},{56,120},{... | collective-permute-start | bytes 835592 | tf_op jit(solution)/shard_map/ppermute | solution.py:36
  89.1 4.9 %collective-permute-done.3 = f32[4,136,128]{2,1,0:T(8,128)S(1)} collective-permute-done((f32[4,136,128]{2,1,0:T(8,128)S(1)}, f32[4,136,128]{2,1,0:T(8,128)S(1)}, u32[]{:S(2)}, u32[]{:S(2)}) %collective-permute-start.3) | collective-permute-done | bytes 278560 | tf_op jit(solution)/shard_map/ppermute | solution.py:36
  95.2 5.2 %collective-permute-start.4 = (f32[4,136,128]{2,1,0:T(8,128)S(1)}, f32[4,136,128]{2,1,0:T(8,128)S(1)}, u32[]{:S(2)}, u32[]{:S(2)}) collective-permute-start(f32[4,136,128]{2,1,0:T(8,128)S(1)} %maximum_maximum_fusion.6), channel_id=1, source_target_pairs={{0,128},{8,136},{16,144},{24,152},{32,160},{40,168},{48,176},{56,1... | collective-permute-start | bytes 835592 | tf_op jit(solution)/shard_map/ppermute | solution.py:36
  100.8 3.8 %collective-permute-done.4 = f32[4,136,128]{2,1,0:T(8,128)S(1)} collective-permute-done((f32[4,136,128]{2,1,0:T(8,128)S(1)}, f32[4,136,128]{2,1,0:T(8,128)S(1)}, u32[]{:S(2)}, u32[]{:S(2)}) %collective-permute-start.4) | collective-permute-done | bytes 278560 | tf_op jit(solution)/shard_map/ppermute | solution.py:36
  106.3 3.1 fusion.8
  112.3 3.8 %scatter_custom_fusion.1 = bf16[768]{0:T(1024)(128)(2,1)S(1)} fusion(s32[512]{0:T(512)S(1)} %bitcast.165, bf16[512]{0:T(512)(128)(2,1)S(1)} %reshape.348, bf16[]{:T(256)} %constant.126.clone.1), kind=kCustom, calls=%fused_computation.150 | custom fusion | bytes 1538 | tf_op jit(solution)/shard_map/scatter | solution.py:125
  116.1 2.6 scatter_custom_fusion
  119.3 30.4 %reduce-scatter.3.cloned.1.call-done = bf16[1,256,384]{2,1,0:T(8,128)(2,1)} async-done(((bf16[8,256,384]{2,1,0:T(8,128)(2,1)}), bf16[1,256,384]{2,1,0:T(8,128)(2,1)}) %reduce-scatter.3.cloned.1.call-update) | async-done | bytes 196624 | tf_op jit(solution)/shard_map/reduce_scatter | solution.py:98
  151.3 3.3 gather_fusion
  154.7 1.8 slice_select_fusion.1
  156.4 2.2 scatter.24
  158.7 11.4 %all-to-all-start.1 = ((bf16[32,24,512]{2,1,0:T(8,128)(2,1)}), bf16[32,24,512]{2,1,0:T(8,128)(2,1)S(1)}, u32[]{:S(2)}, u32[]{:S(2)}) async-start(bf16[32,24,512]{2,1,0:T(8,128)(2,1)} %bitcast.15), calls=%async_computation.2 | async-start | bytes 1572864 | tf_op jit(solution)/shard_map/all_to_all | solution.py:128
  170.2 14.1 %all-to-all-done.1 = bf16[32,24,512]{2,1,0:T(8,128)(2,1)S(1)} async-done(((bf16[32,24,512]{2,1,0:T(8,128)(2,1)}), bf16[32,24,512]{2,1,0:T(8,128)(2,1)S(1)}, u32[]{:S(2)}, u32[]{:S(2)}) %all-to-all-start.1) | async-done | bytes 786464 | tf_op jit(solution)/shard_map/all_to_all | solution.py:128
  185.7 5.0 %copy.212 = bf16[80,8,8,384]{3,2,1,0:T(8,128)(2,1)} copy(bf16[80,8,8,384]{3,1,2,0:T(8,128)(2,1)} %bitcast.152) | data formatting | bytes 7864320
  190.7 50.0 %all-gather.3.cloned.1.call-done = bf16[6208,384]{1,0:T(8,128)(2,1)} async-done(((bf16[776,384]{1,0:T(8,128)(2,1)}), bf16[6208,384]{1,0:T(8,128)(2,1)}) %all-gather.3.cloned.1.call-update) | async-done | bytes 4767760 | tf_op jit(solution)/shard_map/all_gather | solution.py:136
  242.4 7.2 %fusion.76 = f32[768,640,1]{1,0,2:T(8,128)S(1)} fusion(bf16[8,384,640]{2,1,0:T(8,128)(2,1)} %bitcast.176, bf16[8,776,384]{2,1,0:T(8,128)(2,1)} %bitcast.173, f32[8,384]{1,0:T(8,128)S(1)} %bitcast.158, f32[768]{0:T(1024)S(1)} %add_rsqrt_fusion), kind=kOutput, calls=%fused_computation.159 | convolution fusion | flops 3029336064 | bytes 10632192 | tf_op jit(solution)/shard_map/grc,gcf->rf/dot_general | solution.py:156
  249.7 4.0 %fusion.9 = bf16[768,640,1]{1,0,2:T(8,128)(2,1)S(1)} fusion(bf16[8,384,640]{2,1,0:T(8,128)(2,1)S(1)} %bitcast.177, f32[768,640,1]{1,0,2:T(8,128)S(1)} %fusion.76, bf16[8,776,384]{2,1,0:T(8,128)(2,1)S(1)} %bitcast.175, f32[8,384]{1,0:T(8,128)S(1)} %bitcast.159, f32[768]{0:T(1024)S(1)} %add_rsqrt_fusion), kind=kOutput, calls=%fused_computation.18 | convolution fusion | flops 3032285184 | bytes 11616256 | tf_op jit(solution)/shard_map/grc,gcf->rf/dot_general | solution.py:162
  253.8 5.6 %convert_bitcast_fusion = bf16[8,768,384]{2,1,0:T(8,128)(2,1)} fusion(bf16[768,640,1]{1,0,2:T(8,128)(2,1)S(1)} %fusion.9, bf16[640,8,384]{2,1,0:T(8,128)(2,1)S(1)} %bitcast.153), kind=kOutput, calls=%fused_computation.5 | convolution fusion | flops 3022258176 | bytes 9633792 | tf_op jit(solution)/shard_map/rf,fgc->grc/dot_general | solution.py:170
  260.3 4.0 %select_reduce_fusion = (f32[768]{0:T(1024)S(1)}, f32[768]{0:T(1024)S(1)}) fusion(s32[768]{0:T(1024)S(1)} %convert_reduce_fusion, pred[32]{0:T(512)(128)(4,1)S(1)} %iota_compare_fusion.4, bf16[4,8,8,384]{3,2,1,0:T(8,128)(2,1)S(1)} %bitcast.178, bf16[8,776,384]{2,1,0:T(8,128)(2,1)} %bitcast.174, f32[8,384]{1,0:T(8,128)S(1)} %bitcast.160, ...), kind=kOutput, calls=%fused_computation.97 | convolution fusion | flops 160553472 | bytes 4939808 | tf_op jit(solution)/shard_map/grc,gce->re/dot_general | solution.py:147
  265.0 53.6 %reduce-scatter.5.cloned.1.call-done = bf16[1,768,384]{2,1,0:T(8,128)(2,1)} async-done(((bf16[8,768,384]{2,1,0:T(8,128)(2,1)}), bf16[1,768,384]{2,1,0:T(8,128)(2,1)}) %reduce-scatter.5.cloned.1.call-update) | async-done | bytes 589840 | tf_op jit(solution)/shard_map/reduce_scatter | solution.py:173
  318.6 2.2 maximum_maximum_fusion
  320.7 7.6 %all-to-all-start.2 = ((bf16[32,24,512]{2,1,0:T(8,128)(2,1)}), bf16[32,24,512]{2,1,0:T(8,128)(2,1)S(1)}, u32[]{:S(2)}, u32[]{:S(2)}) async-start(bf16[32,24,512]{2,1,0:T(8,128)(2,1)} %maximum_maximum_fusion), calls=%async_computation.4 | async-start | bytes 1572864 | tf_op jit(solution)/shard_map/all_to_all | solution.py:178
  328.3 14.2 %all-to-all-done.2 = bf16[32,24,512]{2,1,0:T(8,128)(2,1)S(1)} async-done(((bf16[32,24,512]{2,1,0:T(8,128)(2,1)}), bf16[32,24,512]{2,1,0:T(8,128)(2,1)S(1)}, u32[]{:S(2)}, u32[]{:S(2)}) %all-to-all-start.2) | async-done | bytes 786464 | tf_op jit(solution)/shard_map/all_to_all | solution.py:178
  342.6 2.0 gather_fusion.1
  (154 shorter events, 31.4 us)
Async XLA Ops:
  6.5 41.2 %copy-start = (bf16[256,512]{1,0:T(8,128)(2,1)S(1)}, bf16[256,512]{1,0:T(8,128)(2,1)}, u32[]{:S(2)}) copy-start(bf16[256,512]{1,0:T(8,128)(2,1)} %param.17) | copy-start | bytes 786436
  6.5 19.5 %copy-start.13 = (bf16[96,512]{1,0:T(8,128)(2,1)S(1)}, bf16[96,512]{1,0:T(8,128)(2,1)}, u32[]{:S(2)}) copy-start(bf16[96,512]{1,0:T(8,128)(2,1)} %param.22) | copy-start | bytes 294916
  10.3 17.8 %copy-start.9 = (bf16[256,512]{0,1:T(8,128)(2,1)}, bf16[256,512]{0,1:T(8,128)(2,1)S(1)}, u32[]{:S(2)}) copy-start(bf16[256,512]{0,1:T(8,128)(2,1)S(1)} %copy.206) | copy-start | bytes 786436
  11.9 8.0 %collective-permute-start = (f32[4,136,128]{2,1,0:T(8,128)S(1)}, f32[4,136,128]{2,1,0:T(8,128)S(1)}, u32[]{:S(2)}, u32[]{:S(2)}) collective-permute-start(f32[4,136,128]{2,1,0:T(8,128)S(1)} %maximum_maximum_fusion.2), channel_id=1, source_target_pairs={{0,8},{8,16},{16,24},{24,32},{32,40},{40,48},{48,56},{56,64},{64,7... | collective-permute-start | bytes 835592 | tf_op jit(solution)/shard_map/ppermute | solution.py:36
  19.9 0.7 copy-start.3
  20.7 0.7 copy-start.5
  22.2 15.7 %collective-permute-start.1 = (f32[4,136,128]{2,1,0:T(8,128)}, f32[4,136,128]{2,1,0:T(8,128)}, u32[]{:S(2)}, u32[]{:S(2)}) collective-permute-start(f32[4,136,128]{2,1,0:T(8,128)} %maximum_maximum_fusion.3), channel_id=1, source_target_pairs={{0,16},{8,24},{16,32},{24,40},{32,48},{40,56},{48,64},{56,72},{64,... | collective-permute-start | bytes 835592 | tf_op jit(solution)/shard_map/ppermute | solution.py:36
  28.0 78.3 %all-to-all-start = ((bf16[32,96,512]{2,1,0:T(8,128)(2,1)}), bf16[32,96,512]{2,1,0:T(8,128)(2,1)S(1)}, u32[]{:S(2)}, u32[]{:S(2)}) async-start(bf16[32,96,512]{2,1,0:T(8,128)(2,1)} %stack.2), calls=%async_computation | async-start | bytes 6291456 | tf_op jit(solution)/shard_map/all_to_all | solution.py:14
  37.6 51.4 %copy-start.15 = (bf16[512]{0:T(512)(128)(2,1)S(1)}, bf16[512]{0:T(512)(128)(2,1)}, u32[]{:S(2)}) copy-start(bf16[512]{0:T(512)(128)(2,1)} %param.21) | copy-start | bytes 3076
  37.7 112.1 %reduce-scatter.3.cloned.1.call-start = ((), (), s32[]{:S(2)}) async-start(), calls=%async_computation.5 | async-start | bytes 1769472 | tf_op jit(solution)/shard_map/reduce_scatter | solution.py:98
  38.9 3.4 copy-start.7
  40.7 0.7 copy-start.6
  42.2 36.2 %collective-permute-start.2 = (f32[4,136,128]{2,1,0:T(8,128)}, f32[4,136,128]{2,1,0:T(8,128)}, u32[]{:S(2)}, u32[]{:S(2)}) collective-permute-start(f32[4,136,128]{2,1,0:T(8,128)} %maximum_maximum_fusion.4), channel_id=1, source_target_pairs={{0,32},{8,40},{16,48},{24,56},{32,64},{40,72},{48,80},{56,88},{64,... | collective-permute-start | bytes 835592 | tf_op jit(solution)/shard_map/ppermute | solution.py:36
  50.1 50.3 %copy-start.4 = (f32[4,136,128]{2,1,0:T(8,128)S(1)}, f32[4,136,128]{2,1,0:T(8,128)}, u32[]{:S(2)}) copy-start(f32[4,136,128]{2,1,0:T(8,128)} %copy-done.3) | copy-start | bytes 835588
  50.1 54.5 %copy-start.1 = (f32[4,136,128]{2,1,0:T(8,128)S(1)}, f32[4,136,128]{2,1,0:T(8,128)}, u32[]{:S(2)}) copy-start(f32[4,136,128]{2,1,0:T(8,128)} %constant.121.clone.1) | copy-start | bytes 835588
  50.1 54.5 %copy-start.8 = (f32[4,136,128]{2,1,0:T(8,128)S(1)}, f32[4,136,128]{2,1,0:T(8,128)}, u32[]{:S(2)}) copy-start(f32[4,136,128]{2,1,0:T(8,128)} %copy-done.7) | copy-start | bytes 835588
  50.1 54.5 %copy-start.12 = (f32[256,4,128]{0,2,1:T(8,128)S(1)}, f32[256,4,128]{0,2,1:T(8,128)}, u32[]{:S(2)}) copy-start(f32[256,4,128]{0,2,1:T(8,128)} %convolution_bitcast_fusion.1) | copy-start | bytes 1572868
  81.3 12.7 %collective-permute-start.3 = (f32[4,136,128]{2,1,0:T(8,128)S(1)}, f32[4,136,128]{2,1,0:T(8,128)S(1)}, u32[]{:S(2)}, u32[]{:S(2)}) collective-permute-start(f32[4,136,128]{2,1,0:T(8,128)S(1)} %maximum_maximum_fusion.5), channel_id=1, source_target_pairs={{0,64},{8,72},{16,80},{24,88},{32,96},{40,104},{48,112},{56,120},{... | collective-permute-start | bytes 835592 | tf_op jit(solution)/shard_map/ppermute | solution.py:36
  95.2 9.4 %collective-permute-start.4 = (f32[4,136,128]{2,1,0:T(8,128)S(1)}, f32[4,136,128]{2,1,0:T(8,128)S(1)}, u32[]{:S(2)}, u32[]{:S(2)}) collective-permute-start(f32[4,136,128]{2,1,0:T(8,128)S(1)} %maximum_maximum_fusion.6), channel_id=1, source_target_pairs={{0,128},{8,136},{16,144},{24,152},{32,160},{40,168},{48,176},{56,1... | collective-permute-start | bytes 835592 | tf_op jit(solution)/shard_map/ppermute | solution.py:36
  105.4 4.0 %copy-start.14 = (s32[256,2]{0,1:T(2,128)S(1)}, s32[256,2]{0,1:T(2,128)}, u32[]{:S(2)}) copy-start(s32[256,2]{0,1:T(2,128)} %param.26) | copy-start | bytes 6148
  151.3 18.8 %copy-start.16 = (bf16[384]{0:T(512)(128)(2,1)S(1)}, bf16[384]{0:T(512)(128)(2,1)}, u32[]{:S(2)}) copy-start(bf16[384]{0:T(512)(128)(2,1)} %param.24) | copy-start | bytes 2308
  158.7 25.6 %all-to-all-start.1 = ((bf16[32,24,512]{2,1,0:T(8,128)(2,1)}), bf16[32,24,512]{2,1,0:T(8,128)(2,1)S(1)}, u32[]{:S(2)}, u32[]{:S(2)}) async-start(bf16[32,24,512]{2,1,0:T(8,128)(2,1)} %bitcast.15), calls=%async_computation.2 | async-start | bytes 1572864 | tf_op jit(solution)/shard_map/all_to_all | solution.py:128
  170.1 70.7 %all-gather.3.cloned.1.call-start = ((), (), s32[]{:S(2)}) async-start(), calls=%async_computation.7 | async-start | bytes 5363712 | tf_op jit(solution)/shard_map/all_gather | solution.py:136
  185.7 132.9 %reduce-scatter.5.cloned.1.call-start = ((), (), s32[]{:S(2)}) async-start(), calls=%async_computation.6 | async-start | bytes 5308416 | tf_op jit(solution)/shard_map/reduce_scatter | solution.py:173
  242.4 7.3 %copy-start.17 = (bf16[6208,384]{1,0:T(8,128)(2,1)S(1)}, bf16[6208,384]{1,0:T(8,128)(2,1)}, u32[]{:S(2)}) copy-start(bf16[6208,384]{1,0:T(8,128)(2,1)} %all-gather.3.cloned.1.call-done) | copy-start | bytes 14303236
  242.4 7.3 %copy-start.18 = (bf16[1,3072,640]{2,1,0:T(8,128)(2,1)S(1)}, bf16[1,3072,640]{2,1,0:T(8,128)(2,1)}, u32[]{:S(2)}) copy-start(bf16[1,3072,640]{2,1,0:T(8,128)(2,1)} %param.28) | copy-start | bytes 11796484
  249.7 4.1 %copy-start.2 = (bf16[80,8,8,384]{3,2,1,0:T(8,128)(2,1)S(1)}, bf16[80,8,8,384]{3,2,1,0:T(8,128)(2,1)}, u32[]{:S(2)}) copy-start(bf16[80,8,8,384]{3,2,1,0:T(8,128)(2,1)} %copy.212) | copy-start | bytes 11796484
  259.4 0.9 copy-start.19
  320.7 21.8 %all-to-all-start.2 = ((bf16[32,24,512]{2,1,0:T(8,128)(2,1)}), bf16[32,24,512]{2,1,0:T(8,128)(2,1)S(1)}, u32[]{:S(2)}, u32[]{:S(2)}) async-start(bf16[32,24,512]{2,1,0:T(8,128)(2,1)} %maximum_maximum_fusion), calls=%async_computation.4 | async-start | bytes 1572864 | tf_op jit(solution)/shard_map/all_to_all | solution.py:178
  342.6 4.4 %copy-start.10 = (bf16[256,384]{1,0:T(8,128)(2,1)S(1)}, bf16[256,384]{1,0:T(8,128)(2,1)}, u32[]{:S(2)}) copy-start(bf16[256,384]{1,0:T(8,128)(2,1)} %param.23) | copy-start | bytes 589828
  342.6 4.4 %copy-start.11 = (bf16[1,256,384]{2,1,0:T(8,128)(2,1)S(1)}, bf16[1,256,384]{2,1,0:T(8,128)(2,1)}, u32[]{:S(2)}) copy-start(bf16[1,256,384]{2,1,0:T(8,128)(2,1)} %reduce-scatter.3.cloned.1.call-done) | copy-start | bytes 589828
Sparse Core Ops, SparseCore 0:
  109.6 40.0 reduce-scatter.2
  185.8 54.9 all-gather.2
  259.5 58.9 reduce-scatter.4
